TPU v7x, 32 devices: a whole 2x2x4 slice. The times are simulated.
32 devices in a mesh: dp: 2 (over x), mp: 16 (over z, y, core).
Axes of the slice: x: 2, y: 2, z: 4, core: 2. Of those that a mesh axis runs over, the one named last changes fastest.
Arguments:
- node_features: bfloat16 [512, 6144], P('mp', 'dp'), may hold values from -6 to 6
- weights_one: bfloat16 [1024, 512], replicated, may hold values from -0.25 to 0.25
- weights_two: bfloat16 [1024, 512], replicated, may hold values from -0.25 to 0.25
- neighbor_owner: int32 [6144, 8], P('dp'), may hold values from 0 to 15, all different within a row; in each aligned block of 192 rows (0 to 191, 192 to 383, ...) at most 144 rows name the same one
- neighbor_row: int32 [6144, 8], P('dp'), may hold values from 0 to 191
- neighbor_count: int32 [6144], P('dp'), may hold values from 4 to 8
- cotangent: bfloat16 [6144, 512], P(('dp', 'mp')), may hold values from -0.076171875 to 0.076171875
Outputs:
- node_output: bfloat16 [6144, 512], P(('dp', 'mp'))
- weight_grads: float32 [2048, 512], P(('dp', 'mp'))
Inputs may be any that keep to these rules, and one draw needn't show every extreme that they name: `neighbor_owner`: each row names 8 different owners; among the rows of one device (aligned blocks of 192 rows) no owner is named more than 144 times, and in some block one owner exactly 144 times. Slots k >= neighbor_count[r] are padding and carry no edge.
All inputs are finite; a program needn't handle non-finite values.
Results may differ from a plain program's by a relative error of at most 0.0052.
Values may be sent and summed in bfloat16 or wider, within the bound.
No kernel may reach another device: no remote copies, remote signals or barrier semaphores. Data moves between devices by JAX's collectives and lax.ppermute only.
A program may use at most 64 MiB of HBM per device.

v0:
```python
import jax
import jax.numpy as jnp
from jax import lax
from jax.sharding import PartitionSpec as P


def column_mean(table, indices, live, inverse):
    total = jnp.zeros((table.shape[0], indices.shape[1]), jnp.float32)
    for slot_index in range(indices.shape[0]):
        picked = jnp.take(table, indices[slot_index], axis=1)
        kept = jnp.where(live[slot_index][None, :], picked, jnp.zeros_like(picked))
        total = total + kept.astype(jnp.float32)
    return (total * inverse[None, :]).astype(jnp.bfloat16)


def silu_slope(values):
    sigmoid = jax.nn.sigmoid(values)
    return sigmoid * (1.0 + values * (1.0 - sigmoid))


def contract(left, right, left_dim, right_dim):
    return lax.dot_general(
        left, right, (((left_dim,), (right_dim,)), ((), ())), preferred_element_type=jnp.float32
    )


def shards(
    node_features, weights_one, weights_two, neighbor_owner, neighbor_row, neighbor_count, cotangent
):
    devices = lax.axis_size("mp")
    own_index = lax.axis_index("mp")
    node_dev = cotangent.shape[0]
    all_nodes = neighbor_owner.shape[0]
    fanout = neighbor_owner.shape[1]
    feat_width = weights_one.shape[0] // 2
    hidden = weights_one.shape[1]
    capacity = 3 * node_dev * fanout // (2 * devices)
    live = lax.broadcasted_iota(jnp.int32, (all_nodes, fanout), 1) < neighbor_count[:, None]
    inverse_all = 1.0 / neighbor_count.astype(jnp.float32)
    owner_ids = lax.broadcasted_iota(jnp.int32, (devices, 1, 1), 0)
    match = (neighbor_owner[None, :, :] == owner_ids) & live[None, :, :]
    rowsel = jnp.max(jnp.where(match, neighbor_row[None, :, :], -1), axis=2)
    has = rowsel >= 0
    with jax.named_scope("layer_one_mean"):
        if all_nodes * all_nodes <= 4096 * 4096:
            row_ids = lax.broadcasted_iota(jnp.int32, (1, node_dev, 1), 1)
            adjacency = (rowsel[:, None, :] == row_ids).astype(jnp.bfloat16)
            adjacency = adjacency.reshape(devices * node_dev, all_nodes)
            summed = contract(node_features, adjacency, 1, 0)
            agg_one_cols = (summed * inverse_all[None, :]).astype(jnp.bfloat16)
        else:
            owner_slots = neighbor_owner.T
            global_ids = owner_slots * node_dev + neighbor_row.T
            agg_one_cols = column_mean(node_features, global_ids, live.T, inverse_all)
    own_feats, own_agg_one = (
        lax.all_to_all(node_features, "mp", split_axis=1, concat_axis=0, tiled=True),
        lax.all_to_all(agg_one_cols, "mp", split_axis=1, concat_axis=0, tiled=True),
    )
    pre_one = contract(weights_one[:feat_width], own_feats, 0, 0) + contract(
        weights_one[feat_width:], own_agg_one, 0, 0
    )
    hidden_one = jax.nn.silu(pre_one).astype(jnp.bfloat16)
    with jax.named_scope("slot_tables"):
        blocks = has.reshape(devices * devices, node_dev).astype(jnp.bfloat16)
        before = (
            lax.broadcasted_iota(jnp.int32, (node_dev, node_dev), 0)
            < lax.broadcasted_iota(jnp.int32, (node_dev, node_dev), 1)
        ).astype(jnp.bfloat16)
        ranks = contract(blocks, before, 1, 0).astype(jnp.int32).reshape(devices, devices, node_dev)
        has_blocks = has.reshape(devices, devices, node_dev)
        rows_blocks = rowsel.reshape(devices, devices, node_dev)
        cap_ids = lax.broadcasted_iota(jnp.int32, (1, capacity, 1), 1)
        own_rank = lax.dynamic_index_in_dim(ranks, own_index, 1, keepdims=False)
        own_has = lax.dynamic_index_in_dim(has_blocks, own_index, 1, keepdims=False)
        gathered = ((own_rank[:, None, :] == cap_ids) & own_has[:, None, :]).astype(jnp.bfloat16)
        gathered = gathered.reshape(devices * capacity, node_dev)
        req_rank = lax.dynamic_index_in_dim(ranks, own_index, 0, keepdims=False)
        req_has = lax.dynamic_index_in_dim(has_blocks, own_index, 0, keepdims=False)
        req_rows = lax.dynamic_index_in_dim(rows_blocks, own_index, 0, keepdims=False)
        pick = ((req_rank[:, None, :] == cap_ids) & req_has[:, None, :]).astype(jnp.bfloat16)
        row_ids = lax.broadcasted_iota(jnp.int32, (1, 1, node_dev), 2)
        which = (req_rows[:, :, None] == row_ids).astype(jnp.bfloat16)
        asked = lax.dot_general(
            pick, which, (((2,), (1,)), ((0,), (0,))), preferred_element_type=jnp.float32
        )
        asked = asked.astype(jnp.bfloat16).reshape(devices * capacity, node_dev)
    own_inverse = lax.dynamic_slice_in_dim(inverse_all, own_index * node_dev, node_dev, 0)
    outgoing = contract(hidden_one, asked, 1, 1).astype(jnp.bfloat16)
    incoming = lax.all_to_all(outgoing, "mp", split_axis=1, concat_axis=1, tiled=True)
    total = contract(incoming, gathered, 1, 0)
    agg_two = (total * own_inverse[None, :]).astype(jnp.bfloat16)
    self_two = weights_two[:hidden]
    neigh_two = weights_two[hidden:]
    node_output = (
        contract(hidden_one, self_two, 0, 0) + contract(agg_two, neigh_two, 0, 0)
    ).astype(jnp.bfloat16)
    down_self = contract(self_two, cotangent, 1, 1)
    down_neigh = (contract(neigh_two, cotangent, 1, 1) * own_inverse[None, :]).astype(jnp.bfloat16)
    outgoing_grad = contract(down_neigh, gathered, 1, 1).astype(jnp.bfloat16)
    incoming_grad = lax.all_to_all(outgoing_grad, "mp", split_axis=1, concat_axis=1, tiled=True)
    neighbor_sum = contract(incoming_grad, asked, 1, 0)
    grad_hidden = down_self + neighbor_sum
    grad_pre = (grad_hidden * silu_slope(pre_one)).astype(jnp.bfloat16)
    terms = jnp.concatenate(
        [
            contract(own_feats, grad_pre, 1, 1),
            contract(own_agg_one, grad_pre, 1, 1),
            contract(hidden_one, cotangent, 1, 0),
            contract(agg_two, cotangent, 1, 0),
        ],
        axis=0,
    )
    weight_grads = lax.psum_scatter(terms, ("dp", "mp"), scatter_dimension=0, tiled=True)
    return (node_output, weight_grads)


def solution(mesh):
    in_specs = (
        P("mp", "dp"),
        P(),
        P(),
        P("dp", None),
        P("dp", None),
        P("dp"),
        P(("dp", "mp"), None),
    )
    out_specs = (P(("dp", "mp"), None), P(("dp", "mp"), None))
    return jax.shard_map(shards, mesh=mesh, in_specs=in_specs, out_specs=out_specs, check_vma=False)
```

profile of v0, /device:TPU:0, one launch (start us, length us, event | category | flops | bytes accessed | tf_op | source)
XLA Modules:
  0.0 325.1 jit_solution(16609977738096543799)
XLA Ops:
  7.2 0.0 copy-start
  7.2 1.3 all_to_all.40
  8.5 0.8 copy.27
  9.3 7.4 %all-to-all-start = ((bf16[32,16,192]{2,0,1:T(8,128)(2,1)}), bf16[32,16,192]{2,0,1:T(8,128)(2,1)S(1)}, u32[]{:S(2)}, u32[]{:S(2)}) async-start(bf16[32,16,192]{2,0,1:T(8,128)(2,1)} %copy.27), calls=%async_computation | async-start | bytes 524288 | tf_op jit(solution)/shard_map/all_to_all | solution.py:56
  16.7 0.7 iota_compare_fusion.9
  17.4 0.7 convert_divide_fusion
  18.1 0.1 eq.95
  18.2 1.8 select_reduce_fusion
  20.0 0.0 copy-start.7
  20.0 9.7 %bitcast_compare_fusion = pred[3072,3072]{1,0:T(32,128)(4,1)} fusion(s32[3072]{0:T(1024)S(1)} %eq.95, s32[16,3072]{1,0:T(8,128)S(1)} %select_reduce_fusion), kind=kLoop, calls=%fused_computation | loop fusion | flops 9437184 | bytes 9646080 | tf_op jit(solution)/shard_map/layer_one_mean/eq | solution.py:47
  29.7 0.2 ge.17
  29.9 0.0 copy-done.7
  29.9 8.5 %fusion.1 = bf16[32,3072]{1,0:T(8,128)(2,1)S(1)} fusion(pred[3072,3072]{1,0:T(32,128)(4,1)} %bitcast_compare_fusion, bf16[32,3072]{1,0:T(8,128)(2,1)S(1)} %copy-done.7, f32[3072]{0:T(1024)S(1)} %convert_divide_fusion), kind=kOutput, calls=%fused_computation.6 | convolution fusion | flops 604176384 | bytes 9842688 | tf_op jit(solution)/shard_map/layer_one_mean/dot_general | solution.py:22
  38.4 0.4 convolution_convert_fusion.2
  38.9 0.1 reduce_max.12
  39.0 0.0 copy-start.1
  39.0 0.3 all_to_all.44
  39.3 0.8 copy.28
  40.1 0.1 copy.29
  40.2 0.0 copy-start.6
  40.3 0.0 all-to-all-done
  40.4 6.1 %all-to-all-start.1 = ((bf16[32,16,192]{2,0,1:T(8,128)(2,1)}), bf16[32,16,192]{2,0,1:T(8,128)(2,1)}, u32[]{:S(2)}, u32[]{:S(2)}) async-start(bf16[32,16,192]{2,0,1:T(8,128)(2,1)} %copy.28), calls=%async_computation.1 | async-start | bytes 524288 | tf_op jit(solution)/shard_map/all_to_all | solution.py:57
  46.5 0.1 dynamic_slice.27
  46.6 0.1 eq.112
  46.7 0.0 copy-done.1
  46.7 0.0 copy-done.6
  46.7 0.5 fusion.8
  47.2 0.0 copy-done
  47.2 2.2 convolution_convert_fusion
  49.4 2.5 copy.31
  51.9 4.6 %all-to-all-done.1 = bf16[32,16,192]{2,0,1:T(8,128)(2,1)} async-done(((bf16[32,16,192]{2,0,1:T(8,128)(2,1)}), bf16[32,16,192]{2,0,1:T(8,128)(2,1)}, u32[]{:S(2)}, u32[]{:S(2)}) %all-to-all-start.1) | async-done | bytes 196640 | tf_op jit(solution)/shard_map/all_to_all | solution.py:57
  56.5 3.7 %all-to-all-start.3 = ((bf16[512,16,144]{0,2,1:T(8,128)(2,1)}), bf16[512,16,144]{0,2,1:T(8,128)(2,1)S(1)}, u32[]{:S(2)}, u32[]{:S(2)}) async-start(bf16[512,16,144]{0,2,1:T(8,128)(2,1)} %bitcast.16), calls=%async_computation.3 | async-start | bytes 4718592 | tf_op jit(solution)/shard_map/all_to_all | solution.py:100
  60.3 0.0 copy-start.2
  60.3 0.8 dynamic-slice_bitcast_fusion
  61.1 1.3 fusion.11
  62.5 0.0 copy-start.8
  62.5 0.0 copy-done.2
  62.5 0.3 fusion.33
  62.8 1.3 fusion.18
  64.1 0.0 copy-done.8
  64.1 2.4 convolution_convert_fusion.1
  66.5 4.3 %copy.30 = bf16[512,2304]{0,1:T(8,128)(2,1)} copy(bf16[512,2304]{1,0:T(8,128)(2,1)} %convolution_convert_fusion.1) | data formatting | bytes 4718592 | tf_op jit(solution)/shard_map/convert_element_type | solution.py:88
  70.8 35.1 %all-to-all-done.3 = bf16[512,16,144]{0,2,1:T(8,128)(2,1)S(1)} async-done(((bf16[512,16,144]{0,2,1:T(8,128)(2,1)}), bf16[512,16,144]{0,2,1:T(8,128)(2,1)S(1)}, u32[]{:S(2)}, u32[]{:S(2)}) %all-to-all-start.3) | async-done | bytes 2359328 | tf_op jit(solution)/shard_map/all_to_all | solution.py:100
  105.9 12.3 %all-to-all-start.2 = ((bf16[512,16,144]{0,2,1:T(8,128)(2,1)}), bf16[512,16,144]{0,2,1:T(8,128)(2,1)}, u32[]{:S(2)}, u32[]{:S(2)}) async-start(bf16[512,16,144]{0,2,1:T(8,128)(2,1)} %bitcast.12), calls=%async_computation.2 | async-start | bytes 4718592 | tf_op jit(solution)/shard_map/all_to_all | solution.py:89
  118.2 0.0 reduce-scatter.2.cloned.1.call-start
  118.2 1.4 fusion.42
  119.6 0.0 copy-start.3
  119.6 2.0 convolution_bitcast_fusion.1
  121.6 0.0 copy-done.3
  121.6 0.4 fusion.29
  122.0 1.2 fusion.43
  123.2 0.3 convolution_bitcast_fusion
  123.5 40.4 %all-to-all-done.2 = bf16[512,16,144]{0,2,1:T(8,128)(2,1)} async-done(((bf16[512,16,144]{0,2,1:T(8,128)(2,1)}), bf16[512,16,144]{0,2,1:T(8,128)(2,1)}, u32[]{:S(2)}, u32[]{:S(2)}) %all-to-all-start.2) | async-done | bytes 2359328 | tf_op jit(solution)/shard_map/all_to_all | solution.py:89
  163.9 0.0 copy-start.5
  163.9 2.6 fusion.26
  166.5 0.3 fusion.44
  166.9 0.0 copy-done.5
  166.9 2.4 pad_maximum_fusion
  169.3 0.0 copy-start.4
  169.3 0.0 reduce-scatter.2.cloned.1.call-update
  169.3 1.2 copy-done.4
  170.5 0.3 fusion.39
  170.8 1.0 fusion.30
  171.7 146.5 %reduce-scatter.2.cloned.1.call-done = f32[64,512]{1,0:T(8,128)} async-done(((f32[2048,512]{1,0:T(8,128)}), f32[64,512]{1,0:T(8,128)}) %reduce-scatter.2.cloned.1.call-update) | async-done | bytes 131088 | tf_op jit(solution)/shard_map/reduce_scatter | solution.py:113
  (9 shorter events, 0.2 us)
Async XLA Ops:
  7.2 40.0 %copy-start = (bf16[192,512]{1,0:T(8,128)(2,1)S(1)}, bf16[192,512]{1,0:T(8,128)(2,1)}, u32[]{:S(2)}) copy-start(bf16[192,512]{1,0:T(8,128)(2,1)} %param.13) | copy-start | bytes 589828
  9.3 31.1 %all-to-all-start = ((bf16[32,16,192]{2,0,1:T(8,128)(2,1)}), bf16[32,16,192]{2,0,1:T(8,128)(2,1)S(1)}, u32[]{:S(2)}, u32[]{:S(2)}) async-start(bf16[32,16,192]{2,0,1:T(8,128)(2,1)} %copy.27), calls=%async_computation | async-start | bytes 524288 | tf_op jit(solution)/shard_map/all_to_all | solution.py:56
  20.0 9.9 %copy-start.7 = (bf16[32,3072]{1,0:T(8,128)(2,1)S(1)}, bf16[32,3072]{1,0:T(8,128)(2,1)}, u32[]{:S(2)}) copy-start(bf16[32,3072]{1,0:T(8,128)(2,1)} %param.7) | copy-start | bytes 589828
  39.0 7.7 %copy-start.1 = (s32[16,16,192]{2,1,0:T(8,128)}, s32[16,16,192]{2,1,0:T(8,128)S(1)}, u32[]{:S(2)}) copy-start(s32[16,16,192]{2,1,0:T(8,128)S(1)} %reduce_max.12) | copy-start | bytes 589828
  40.2 6.4 %copy-start.6 = (s32[256,192]{1,0:T(8,128)}, s32[256,192]{1,0:T(8,128)S(1)}, u32[]{:S(2)}) copy-start(s32[256,192]{1,0:T(8,128)S(1)} %copy.29) | copy-start | bytes 589828
  40.4 16.2 %all-to-all-start.1 = ((bf16[32,16,192]{2,0,1:T(8,128)(2,1)}), bf16[32,16,192]{2,0,1:T(8,128)(2,1)}, u32[]{:S(2)}, u32[]{:S(2)}) async-start(bf16[32,16,192]{2,0,1:T(8,128)(2,1)} %copy.28), calls=%async_computation.1 | async-start | bytes 524288 | tf_op jit(solution)/shard_map/all_to_all | solution.py:57
  56.5 49.3 %all-to-all-start.3 = ((bf16[512,16,144]{0,2,1:T(8,128)(2,1)}), bf16[512,16,144]{0,2,1:T(8,128)(2,1)S(1)}, u32[]{:S(2)}, u32[]{:S(2)}) async-start(bf16[512,16,144]{0,2,1:T(8,128)(2,1)} %bitcast.16), calls=%async_computation.3 | async-start | bytes 4718592 | tf_op jit(solution)/shard_map/all_to_all | solution.py:100
  60.3 2.2 copy-start.2
  62.5 1.7 copy-start.8
  105.9 58.0 %all-to-all-start.2 = ((bf16[512,16,144]{0,2,1:T(8,128)(2,1)}), bf16[512,16,144]{0,2,1:T(8,128)(2,1)}, u32[]{:S(2)}, u32[]{:S(2)}) async-start(bf16[512,16,144]{0,2,1:T(8,128)(2,1)} %bitcast.12), calls=%async_computation.2 | async-start | bytes 4718592 | tf_op jit(solution)/shard_map/all_to_all | solution.py:89
  118.2 200.1 %reduce-scatter.2.cloned.1.call-start = ((), (), s32[]{:S(2)}) async-start(), calls=%async_computation.5 | async-start | bytes 4325376 | tf_op jit(solution)/shard_map/reduce_scatter | solution.py:113
  119.6 2.0 copy-start.3
  163.9 3.0 copy-start.5
  169.3 1.2 copy-start.4
Sparse Core Ops, SparseCore 0:
  169.4 148.7 reduce-scatter.1
where the time goes:
time: 326 us; the launch traced here: 325 us
  waiting for transfers between devices  227 us (70%)
  starting transfers between devices  29.5 us (9%)
  matrix products  25.9 us (8%)
  other arithmetic  15.9 us (5%)
  between operations  14.4 us (4%)
  local copies, waits for them, and re-layouts  12.7 us (4%)
    reduce_scatter x1, waiting for transfers between devices, shards(): lax.psum_scatter(terms, ('dp', 'mp'), scatter_dimension=0, tiled=True)  147 us
    all_to_all x1, waiting for transfers between devices, shards(): lax.all_to_all(outgoing, 'mp', split_axis=1, concat_axis=1, tiled=True)  40.4 us
    all_to_all x1, waiting for transfers between devices, shards(): lax.all_to_all(outgoing_grad, 'mp', split_axis=1, concat_axis=1, tiled=True)  35.1 us
    dot_general x15, matrix products, contract(): lax.dot_general(left, right, (((left_dim,), (right_dim,)), ((), ())), pre...  24.6 us
    all_to_all x1, starting transfers between devices, shards(): lax.all_to_all(outgoing, 'mp', split_axis=1, concat_axis=1, tiled=True)  12.3 us
    eq x1, other arithmetic, shards(): adjacency = (rowsel[:, None, :] == row_ids).astype(jnp.bfloat16)  9.7 us
    all_to_all x1, starting transfers between devices, shards(): lax.all_to_all(node_features, 'mp', split_axis=1, concat_axis=0, tiled=True)  7.39 us
  transfers between devices with their start and end apart: 5, of which 4 were waited for; matrix products, arithmetic and copies ran while one was open for 14% of the time, Pallas kernels for 0%

commit v1 on v0

--- a/solution.py
+++ b/solution.py
@@ -53,7 +53,15 @@
             global_ids = owner_slots * node_dev + neighbor_row.T
             agg_one_cols = column_mean(node_features, global_ids, live.T, inverse_all)
     own_feats, own_agg_one = (
-        lax.all_to_all(node_features, "mp", split_axis=1, concat_axis=0, tiled=True),
+        jnp.concatenate(
+            lax.all_to_all(
+                jnp.stack(jnp.split(node_features, lax.axis_size("mp"), 1), axis=0),
+                axis_name="mp",
+                split_axis=0,
+                concat_axis=0,
+            ),
+            0,
+        ),
         lax.all_to_all(agg_one_cols, "mp", split_axis=1, concat_axis=0, tiled=True),
     )
     pre_one = contract(weights_one[:feat_width], own_feats, 0, 0) + contract(

time: 326 us -> 346 us (1.061)
  local copies, waits for them, and re-layouts: 12.7 us -> 32.5 us
    unnamed x20 -> x35, local copies, waits for them, and re-layouts: 1.25 us -> 21.8 us
  transfers between devices with their start and end apart: 5 -> 5, of which waited for: 4 -> 4; matrix products, arithmetic and copies ran while one was open for 14% -> 13% of each run, Pallas kernels for 0% -> 0%
where the time goes in v1:
time: 346 us; the launch traced here: 345 us
  waiting for transfers between devices  226 us (65%)
  local copies, waits for them, and re-layouts  32.5 us (9%)
  starting transfers between devices  29.5 us (9%)
  matrix products  26 us (8%)
  other arithmetic  15.9 us (5%)
  between operations  14.4 us (4%)
    reduce_scatter x1, waiting for transfers between devices, shards(): lax.psum_scatter(terms, ('dp', 'mp'), scatter_dimension=0, tiled=True)  146 us
    all_to_all x1, waiting for transfers between devices, shards(): lax.all_to_all(outgoing, 'mp', split_axis=1, concat_axis=1, tiled=True)  40.4 us
    all_to_all x1, waiting for transfers between devices, shards(): lax.all_to_all(outgoing_grad, 'mp', split_axis=1, concat_axis=1, tiled=True)  35.1 us
    dot_general x15, matrix products, contract(): lax.dot_general(left, right, (((left_dim,), (right_dim,)), ((), ())), pre...  24.6 us
    unnamed x35, local copies, waits for them, and re-layouts  21.8 us
    all_to_all x1, starting transfers between devices, shards(): lax.all_to_all(outgoing, 'mp', split_axis=1, concat_axis=1, tiled=True)  12.3 us
    eq x1, other arithmetic, shards(): adjacency = (rowsel[:, None, :] == row_ids).astype(jnp.bfloat16)  9.7 us
    all_to_all x1, starting transfers between devices, shards(): lax.all_to_all(jnp.stack(jnp.split(node_features, lax.axis_size('mp'), 1)...  7.39 us
  transfers between devices with their start and end apart: 5, of which 4 were waited for; matrix products, arithmetic and copies ran while one was open for 13% of the time, Pallas kernels for 0%

profile of v1, /device:TPU:0, one launch (start us, length us, event | category | flops | bytes accessed | tf_op | source)
XLA Modules:
  0.0 344.5 jit_solution(594095591588740748)
XLA Ops:
  7.2 0.0 copy-start
  7.2 1.4 constant_dynamic-update-slice_fusion.15
  8.5 1.4 constant_dynamic-update-slice_fusion.14
  9.9 1.4 constant_dynamic-update-slice_fusion.13
  11.3 1.4 constant_dynamic-update-slice_fusion.12
  12.7 1.3 constant_dynamic-update-slice_fusion.11
  14.0 1.4 constant_dynamic-update-slice_fusion.10
  15.4 1.3 constant_dynamic-update-slice_fusion.9
  16.8 1.4 constant_dynamic-update-slice_fusion.8
  18.2 1.3 constant_dynamic-update-slice_fusion.7
  19.5 1.4 constant_dynamic-update-slice_fusion.6
  20.9 1.3 constant_dynamic-update-slice_fusion.5
  22.2 1.4 constant_dynamic-update-slice_fusion.4
  23.6 1.3 constant_dynamic-update-slice_fusion.3
  25.0 1.4 constant_dynamic-update-slice_fusion.2
  26.4 1.3 constant_dynamic-update-slice_fusion.1
  27.7 1.4 constant_dynamic-update-slice_fusion
  29.1 7.4 %all-to-all-start = ((bf16[16,32,192]{2,1,0:T(8,128)(2,1)}), bf16[16,32,192]{2,1,0:T(8,128)(2,1)S(1)}, u32[]{:S(2)}, u32[]{:S(2)}) async-start(bf16[16,32,192]{2,1,0:T(8,128)(2,1)} %constant_dynamic-update-slice_fusion), calls=%async_computation | async-start | bytes 524288 | tf_op jit(solution)/shard_map/all_to_all | solution.py:57
  36.5 0.7 iota_compare_fusion.9
  37.2 0.7 convert_divide_fusion
  37.9 0.1 eq.95
  38.0 1.8 select_reduce_fusion
  39.8 0.0 copy-start.6
  39.8 9.7 %bitcast_compare_fusion = pred[3072,3072]{1,0:T(32,128)(4,1)} fusion(s32[3072]{0:T(1024)S(1)} %eq.95, s32[16,3072]{1,0:T(8,128)S(1)} %select_reduce_fusion), kind=kLoop, calls=%fused_computation | loop fusion | flops 9437184 | bytes 9646080 | tf_op jit(solution)/shard_map/layer_one_mean/eq | solution.py:47
  49.5 0.2 ge.17
  49.7 8.5 %fusion.1 = bf16[32,3072]{1,0:T(8,128)(2,1)S(1)} fusion(pred[3072,3072]{1,0:T(32,128)(4,1)} %bitcast_compare_fusion, bf16[32,3072]{1,0:T(8,128)(2,1)S(1)} %copy-done.6, f32[3072]{0:T(1024)S(1)} %convert_divide_fusion), kind=kOutput, calls=%fused_computation.6 | convolution fusion | flops 604176384 | bytes 9842688 | tf_op jit(solution)/shard_map/layer_one_mean/dot_general | solution.py:22
  58.3 0.4 convolution_convert_fusion.2
  58.7 0.1 reduce_max.12
  58.8 0.3 all_to_all.30
  59.1 0.8 copy.25
  59.9 0.1 copy.26
  60.2 0.0 all-to-all-done
  60.2 6.1 %all-to-all-start.1 = ((bf16[32,16,192]{2,0,1:T(8,128)(2,1)}), bf16[32,16,192]{2,0,1:T(8,128)(2,1)}, u32[]{:S(2)}, u32[]{:S(2)}) async-start(bf16[32,16,192]{2,0,1:T(8,128)(2,1)} %copy.25), calls=%async_computation.1 | async-start | bytes 524288 | tf_op jit(solution)/shard_map/all_to_all | solution.py:65
  66.3 0.1 dynamic_slice.27
  66.4 0.1 eq.112
  66.5 0.5 fusion.8
  67.0 2.2 convolution_convert_fusion
  69.2 2.5 copy.28
  71.7 4.6 %all-to-all-done.1 = bf16[32,16,192]{2,0,1:T(8,128)(2,1)} async-done(((bf16[32,16,192]{2,0,1:T(8,128)(2,1)}), bf16[32,16,192]{2,0,1:T(8,128)(2,1)}, u32[]{:S(2)}, u32[]{:S(2)}) %all-to-all-start.1) | async-done | bytes 196640 | tf_op jit(solution)/shard_map/all_to_all | solution.py:65
  76.3 3.7 %all-to-all-start.3 = ((bf16[512,16,144]{0,2,1:T(8,128)(2,1)}), bf16[512,16,144]{0,2,1:T(8,128)(2,1)S(1)}, u32[]{:S(2)}, u32[]{:S(2)}) async-start(bf16[512,16,144]{0,2,1:T(8,128)(2,1)} %bitcast.31), calls=%async_computation.3 | async-start | bytes 4718592 | tf_op jit(solution)/shard_map/all_to_all | solution.py:108
  80.1 0.0 copy-start.2
  80.1 0.8 dynamic-slice_bitcast_fusion
  80.9 1.3 fusion.11
  82.3 0.3 fusion.33
  82.6 1.3 fusion.21
  83.9 2.4 convolution_convert_fusion.1
  86.3 4.3 %copy.27 = bf16[512,2304]{0,1:T(8,128)(2,1)} copy(bf16[512,2304]{1,0:T(8,128)(2,1)} %convolution_convert_fusion.1) | data formatting | bytes 4718592 | tf_op jit(solution)/shard_map/convert_element_type | solution.py:96
  90.6 35.1 %all-to-all-done.3 = bf16[512,16,144]{0,2,1:T(8,128)(2,1)S(1)} async-done(((bf16[512,16,144]{0,2,1:T(8,128)(2,1)}), bf16[512,16,144]{0,2,1:T(8,128)(2,1)S(1)}, u32[]{:S(2)}, u32[]{:S(2)}) %all-to-all-start.3) | async-done | bytes 2359328 | tf_op jit(solution)/shard_map/all_to_all | solution.py:108
  125.7 12.3 %all-to-all-start.2 = ((bf16[512,16,144]{0,2,1:T(8,128)(2,1)}), bf16[512,16,144]{0,2,1:T(8,128)(2,1)}, u32[]{:S(2)}, u32[]{:S(2)}) async-start(bf16[512,16,144]{0,2,1:T(8,128)(2,1)} %bitcast.27), calls=%async_computation.2 | async-start | bytes 4718592 | tf_op jit(solution)/shard_map/all_to_all | solution.py:97
  138.0 0.0 reduce-scatter.2.cloned.1.call-start
  138.0 1.3 fusion.42
  139.4 2.0 convolution_bitcast_fusion
  141.4 0.4 fusion.29
  141.8 1.2 fusion.44
  143.0 0.3 fusion.43
  143.3 40.4 %all-to-all-done.2 = bf16[512,16,144]{0,2,1:T(8,128)(2,1)} async-done(((bf16[512,16,144]{0,2,1:T(8,128)(2,1)}), bf16[512,16,144]{0,2,1:T(8,128)(2,1)}, u32[]{:S(2)}, u32[]{:S(2)}) %all-to-all-start.2) | async-done | bytes 2359328 | tf_op jit(solution)/shard_map/all_to_all | solution.py:97
  183.7 2.6 fusion.26
  186.3 0.3 fusion.45
  186.7 2.4 pad_maximum_fusion
  189.1 0.0 reduce-scatter.2.cloned.1.call-update
  189.1 1.2 copy-done.4
  190.3 0.3 fusion.39
  190.6 1.0 fusion.30
  191.5 146.1 %reduce-scatter.2.cloned.1.call-done = f32[64,512]{1,0:T(8,128)} async-done(((f32[2048,512]{1,0:T(8,128)}), f32[64,512]{1,0:T(8,128)}) %reduce-scatter.2.cloned.1.call-update) | async-done | bytes 131088 | tf_op jit(solution)/shard_map/reduce_scatter | solution.py:121
  (23 shorter events, 0.2 us)
Async XLA Ops:
  7.2 59.8 %copy-start = (bf16[192,512]{1,0:T(8,128)(2,1)S(1)}, bf16[192,512]{1,0:T(8,128)(2,1)}, u32[]{:S(2)}) copy-start(bf16[192,512]{1,0:T(8,128)(2,1)} %param.13) | copy-start | bytes 589828
  29.1 31.1 %all-to-all-start = ((bf16[16,32,192]{2,1,0:T(8,128)(2,1)}), bf16[16,32,192]{2,1,0:T(8,128)(2,1)S(1)}, u32[]{:S(2)}, u32[]{:S(2)}) async-start(bf16[16,32,192]{2,1,0:T(8,128)(2,1)} %constant_dynamic-update-slice_fusion), calls=%async_computation | async-start | bytes 524288 | tf_op jit(solution)/shard_map/all_to_all | solution.py:57
  39.8 9.9 %copy-start.6 = (bf16[32,3072]{1,0:T(8,128)(2,1)S(1)}, bf16[32,3072]{1,0:T(8,128)(2,1)}, u32[]{:S(2)}) copy-start(bf16[32,3072]{1,0:T(8,128)(2,1)} %param.7) | copy-start | bytes 589828
  58.8 7.7 %copy-start.1 = (s32[16,16,192]{2,1,0:T(8,128)}, s32[16,16,192]{2,1,0:T(8,128)S(1)}, u32[]{:S(2)}) copy-start(s32[16,16,192]{2,1,0:T(8,128)S(1)} %reduce_max.12) | copy-start | bytes 589828
  60.1 6.4 %copy-start.7 = (s32[256,192]{1,0:T(8,128)}, s32[256,192]{1,0:T(8,128)S(1)}, u32[]{:S(2)}) copy-start(s32[256,192]{1,0:T(8,128)S(1)} %copy.26) | copy-start | bytes 589828
  60.2 16.2 %all-to-all-start.1 = ((bf16[32,16,192]{2,0,1:T(8,128)(2,1)}), bf16[32,16,192]{2,0,1:T(8,128)(2,1)}, u32[]{:S(2)}, u32[]{:S(2)}) async-start(bf16[32,16,192]{2,0,1:T(8,128)(2,1)} %copy.25), calls=%async_computation.1 | async-start | bytes 524288 | tf_op jit(solution)/shard_map/all_to_all | solution.py:65
  76.3 49.3 %all-to-all-start.3 = ((bf16[512,16,144]{0,2,1:T(8,128)(2,1)}), bf16[512,16,144]{0,2,1:T(8,128)(2,1)S(1)}, u32[]{:S(2)}, u32[]{:S(2)}) async-start(bf16[512,16,144]{0,2,1:T(8,128)(2,1)} %bitcast.31), calls=%async_computation.3 | async-start | bytes 4718592 | tf_op jit(solution)/shard_map/all_to_all | solution.py:108
  80.1 2.2 copy-start.2
  82.3 1.7 copy-start.8
  125.7 58.0 %all-to-all-start.2 = ((bf16[512,16,144]{0,2,1:T(8,128)(2,1)}), bf16[512,16,144]{0,2,1:T(8,128)(2,1)}, u32[]{:S(2)}, u32[]{:S(2)}) async-start(bf16[512,16,144]{0,2,1:T(8,128)(2,1)} %bitcast.27), calls=%async_computation.2 | async-start | bytes 4718592 | tf_op jit(solution)/shard_map/all_to_all | solution.py:97
  138.0 199.7 %reduce-scatter.2.cloned.1.call-start = ((), (), s32[]{:S(2)}) async-start(), calls=%async_computation.5 | async-start | bytes 4325376 | tf_op jit(solution)/shard_map/reduce_scatter | solution.py:121
  139.4 2.0 copy-start.3
  183.7 3.0 copy-start.5
  189.1 1.2 copy-start.4
Sparse Core Ops, SparseCore 0:
  189.2 148.4 reduce-scatter.1
